TPU v7x, 128 devices: a whole 4x4x4 slice. The times are simulated.
128 devices in a mesh: band: 32 (over z, x, core), seg: 4 (over y).
Axes of the slice: x: 4, y: 4, z: 4, core: 2. Of those that a mesh axis runs over, the one named last changes fastest.
Arguments:
- voltages: float32 [4, 1, 2, 2, 1024, 3072], P('seg', None, None, None, 'band'), may hold values from -6 to 6
- chirp_phase: float32 [1, 1024, 4096], P(None, 'seg', 'band'), may hold values from -3.140625 to 3.140625
Outputs:
- dedispersed: float32 [4, 1, 2, 2, 1024, 3072], P('seg', None, None, None, 'band')
All inputs are finite; a program needn't handle non-finite values.
Results may differ from a plain program's by a relative error of at most 0.00015.
Values sent between devices are 32-bit elements; how exact they have to be, the bound alone decides.
No kernel may reach another device: no remote copies, remote signals or barrier semaphores. Data moves between devices by JAX's collectives and lax.ppermute only.
A program may use at most 64 MiB of HBM per device.

v0:
```python
import math
import jax
import jax.numpy as jnp
from jax import lax
from jax.sharding import PartitionSpec as P


def passed_along(block, axis, distance):
    devices = range(lax.axis_size(axis))
    route = [(i - distance, i) for i in devices if i - distance in devices]
    return lax.ppermute(block, axis, route)


def gathered(block, axis, dim):
    size = lax.axis_size(axis)
    pieces = [block]
    for shift in range(1, size):
        route = [((i + shift) % size, i) for i in range(size)]
        pieces.append(lax.ppermute(block, axis, route))
    ahead = jnp.stack(pieces, axis=0)
    ordered = jnp.roll(ahead, lax.axis_index(axis), axis=0)
    ordered = jnp.moveaxis(ordered, 0, dim)
    shape = list(block.shape)
    shape[dim] *= size
    return ordered.reshape(shape)


def split_factor(length):
    factor = int(math.isqrt(length))
    while length % factor:
        factor -= 1
    return factor


def tables(length, direction):
    places = jnp.arange(length, dtype=jnp.int32)
    product = places[:, None] * places[None, :] % length
    angles = direction * 2.0 * math.pi / length * product.astype(jnp.float32)
    return (jnp.cos(angles), jnp.sin(angles))


def rotate(real_part, imag_part, product, scale):
    angles = scale * product.astype(jnp.float32)
    cosine = jnp.cos(angles)
    sine = jnp.sin(angles)
    return (real_part * cosine - imag_part * sine, real_part * sine + imag_part * cosine)


def transform_last(real_part, imag_part, direction):
    length = real_part.shape[-1]
    inner = split_factor(length)
    outer = length // inner
    leading = real_part.shape[:-1]
    real_part = real_part.reshape(leading + (outer, inner))
    imag_part = imag_part.reshape(leading + (outer, inner))
    cos_outer, sin_outer = tables(outer, direction)
    highest = lax.Precision.HIGHEST
    first_real = jnp.einsum(
        "...nj,nk->...kj", real_part, cos_outer, precision=highest
    ) - jnp.einsum("...nj,nk->...kj", imag_part, sin_outer, precision=highest)
    first_imag = jnp.einsum(
        "...nj,nk->...kj", real_part, sin_outer, precision=highest
    ) + jnp.einsum("...nj,nk->...kj", imag_part, cos_outer, precision=highest)
    outer_index = jnp.arange(outer, dtype=jnp.int32)[:, None]
    inner_index = jnp.arange(inner, dtype=jnp.int32)[None, :]
    first_real, first_imag = rotate(
        first_real,
        first_imag,
        outer_index * inner_index % length,
        direction * 2.0 * math.pi / length,
    )
    cos_inner, sin_inner = tables(inner, direction)
    last_real = jnp.matmul(first_real, cos_inner, precision=highest) - jnp.matmul(
        first_imag, sin_inner, precision=highest
    )
    last_imag = jnp.matmul(first_real, sin_inner, precision=highest) + jnp.matmul(
        first_imag, cos_inner, precision=highest
    )
    last_real = jnp.swapaxes(last_real, -1, -2).reshape(leading + (length,))
    last_imag = jnp.swapaxes(last_imag, -1, -2).reshape(leading + (length,))
    return (last_real, last_imag)


def transform_rows(real_part, imag_part, direction):
    result_real, result_imag = transform_last(
        jnp.swapaxes(real_part, -1, -2), jnp.swapaxes(imag_part, -1, -2), direction
    )
    return (jnp.swapaxes(result_real, -1, -2), jnp.swapaxes(result_imag, -1, -2))


def row_pass(spread):
    result_real, result_imag = transform_rows(spread[:, :, 0], spread[:, :, 1], -1.0)
    return jnp.stack([result_real, result_imag], axis=2)


def column_pass(gathered):
    cols = gathered.shape[-1]
    length_scale = 1.0 / (gathered.shape[-2] * lax.axis_size("band") * cols)
    result_real, result_imag = transform_last(gathered[:, :, 0], gathered[:, :, 1], 1.0)
    result = jnp.stack([result_real * length_scale, result_imag * length_scale], axis=2)
    return result[..., cols // 4 :]


def per_device(voltages, chirp_phase):
    block = voltages[0]
    rows_dev = block.shape[3]
    valid_cols = block.shape[4]
    cols = valid_cols * 4 // 3
    bands = lax.axis_size("band")
    rows = rows_dev * bands
    length = rows * cols
    width = cols // bands
    tail = block[..., valid_cols - cols // 4 :]
    history = passed_along(tail, "seg", 1)
    buffer = jnp.concatenate([history, block], axis=-1)
    real_part, imag_part = transform_last(buffer[:, :, 0], buffer[:, :, 1], -1.0)
    row_index = lax.axis_index("band") * rows_dev + jnp.arange(rows_dev, dtype=jnp.int32)
    col_index = jnp.arange(cols, dtype=jnp.int32)
    real_part, imag_part = rotate(
        real_part,
        imag_part,
        row_index[:, None] * col_index[None, :] % length,
        -2.0 * math.pi / length,
    )
    stacked = jnp.stack([real_part, imag_part], axis=2)
    spectra = row_pass(lax.all_to_all(stacked, "band", split_axis=4, concat_axis=3, tiled=True))
    real_part, imag_part = (spectra[:, :, 0], spectra[:, :, 1])
    phases = gathered(chirp_phase, "seg", 1)
    cosine = jnp.cos(phases)[:, None]
    sine = jnp.sin(phases)[:, None]
    real_part, imag_part = (
        real_part * cosine - imag_part * sine,
        real_part * sine + imag_part * cosine,
    )
    real_part, imag_part = transform_rows(real_part, imag_part, 1.0)
    full_rows = jnp.arange(rows, dtype=jnp.int32)
    own_cols = lax.axis_index("band") * width + jnp.arange(width, dtype=jnp.int32)
    real_part, imag_part = rotate(
        real_part,
        imag_part,
        full_rows[:, None] * own_cols[None, :] % length,
        2.0 * math.pi / length,
    )
    columns = jnp.stack([real_part, imag_part], axis=2)
    result = column_pass(lax.all_to_all(columns, "band", split_axis=3, concat_axis=4, tiled=True))
    return result[None]


def solution(mesh):
    in_specs = (P("seg", None, None, None, "band", None), P(None, "seg", "band"))
    out_specs = P("seg", None, None, None, "band", None)
    return jax.shard_map(
        per_device, mesh=mesh, in_specs=in_specs, out_specs=out_specs, check_vma=False
    )
```

profile of v0, /device:TPU:8, one launch (start us, length us, event | category | flops | bytes accessed | tf_op | source)
XLA Modules:
  0.0 270.5 jit_solution(694913317675415932)
XLA Ops:
  0.4 2.7 collective-permute-start.2
  8.0 3.3 %fusion.81 = (f32[32,4096]{1,0:T(8,128)}, f32[32,4096]{1,0:T(8,128)}) fusion(s32[32]{0:T(128)S(1)} %iota_add_fusion.1), kind=kLoop, calls=%fused_computation.117 | loop fusion | flops 1835008 | bytes 1048704 | tf_op jit(solution)/shard_map/cos | solution.py:44
  11.4 2.9 %fusion.79 = (f32[1024,128]{1,0:T(8,128)}, f32[1024,128]{1,0:T(8,128)}) fusion(s32[128]{0:T(128)S(1)} %iota_add_fusion), kind=kLoop, calls=%fused_computation.115 | loop fusion | flops 1835008 | bytes 1049088 | tf_op jit(solution)/shard_map/cos | solution.py:44
  14.3 7.1 %collective-permute-done = f32[1,2,2,32,1024]{4,3,2,1,0:T(8,128)} collective-permute-done((f32[1,2,2,32,1024]{4,3,2,1,0:T(8,128)S(1)}, f32[1,2,2,32,1024]{4,3,2,1,0:T(8,128)}, u32[]{:S(2)}, u32[]{:S(2)}) %collective-permute-start) | collective-permute-done | bytes 524320 | tf_op jit(solution)/shard_map/ppermute | solution.py:11
  23.6 2.5 reshape.541
  26.1 3.3 %fusion.92 = f32[64,2,32,64]{3,0,2,1:T(8,128)} fusion(f32[2,32,64,64]{3,2,1,0:T(8,128)S(1)} %reshape.541), kind=kOutput, calls=%fused_computation.141 | convolution fusion | flops 201383936 | bytes 2097152 | tf_op jit(solution)/shard_map/...nj,nk->...kj/dot_general | solution.py:60
  29.4 3.4 %fusion.96 = f32[64,2,32,64]{3,0,2,1:T(8,128)} fusion(f32[2,32,64,64]{3,2,1,0:T(8,128)S(1)} %reshape.541), kind=kOutput, calls=%fused_computation.145 | convolution fusion | flops 201383936 | bytes 2097152 | tf_op jit(solution)/shard_map/...nj,nk->...kj/dot_general | solution.py:63
  35.0 4.4 %convolution_subtract_fusion.1 = f32[64,2,32,64]{3,0,2,1:T(8,128)S(1)} fusion(f32[64,2,32,64]{3,0,2,1:T(8,128)} %fusion.92, f32[2,32,64,64]{3,2,1,0:T(8,128)} %reshape.540), kind=kOutput, calls=%fused_computation.39 | convolution fusion | flops 201646080 | bytes 3145728 | tf_op jit(solution)/shard_map/...nj,nk->...kj/dot_general | solution.py:58
  43.6 3.5 %fusion.10 = f32[2,32,64,64]{3,2,1,0:T(8,128)} fusion(f32[64,2,32,64]{3,0,2,1:T(8,128)S(1)} %convolution_add_fusion.1, f32[64,2,32,64]{3,0,2,1:T(8,128)S(1)} %convolution_subtract_fusion.1, f32[64,64]{1,0:T(8,128)S(1)} %get-tuple-element.25, f32[64,64]{1,0:T(8,128)S(1)} %get-tuple-element.26), kind=kOutput, calls=%fused_computation.18 | convolution fusion | flops 202170368 | bytes 3178496 | tf_op jit(solution)/shard_map/dot_general | solution.py:76
  47.1 3.4 %subtract_bitcast_fusion = f32[1,2,32,64,64]{3,4,2,1,0:T(8,128)} fusion(f32[2,32,64,64]{3,2,1,0:T(8,128)S(1)} %fusion.12, f32[64,2,32,64]{3,0,2,1:T(8,128)S(1)} %convolution_add_fusion.1, f32[64,2,32,64]{3,0,2,1:T(8,128)S(1)} %convolution_subtract_fusion.1, f32[64,64]{1,0:T(8,128)S(1)} %get-tuple-element.25, f32[64,64]{1,0:T(8,128)S(1)} %get-tuple-element.26), kind=kOutput, calls=%fused_computation.35 | convolution fusion | flops 202432512 | bytes 4227072 | tf_op jit(solution)/shard_map/dot_general | solution.py:73
  50.5 3.0 %copy.119 = f32[1,2,32,64,64]{4,3,2,1,0:T(8,128)} copy(f32[1,2,32,64,64]{3,4,2,1,0:T(8,128)} %subtract_bitcast_fusion) | data formatting | bytes 2097152 | tf_op jit(solution)/shard_map/transpose | solution.py:79
  55.6 5.5 %add_bitcast_fusion = f32[1,2,32,64,64]{3,4,2,1,0:T(8,128)} fusion(f32[2,32,64,64]{3,2,1,0:T(8,128)} %fusion.10, f32[64,2,32,64]{3,0,2,1:T(8,128)} %copy-done, f32[64,2,32,64]{3,0,2,1:T(8,128)S(1)} %convolution_subtract_fusion.1, f32[64,64]{1,0:T(8,128)S(1)} %get-tuple-element.25, f32[64,64]{1,0:T(8,128)S(1)} %get-tuple-element.26), kind=kOutput, calls=%fused_computation.34 | convolution fusion | flops 202432512 | bytes 4227072 | tf_op jit(solution)/shard_map/dot_general | solution.py:76
  66.6 8.4 %copy.121 = f32[1,2,2,32,4096]{3,1,2,0,4:T(2,128)} copy(f32[1,2,2,32,4096]{4,3,1,2,0:T(8,128)S(1)} %pad_maximum_fusion) | data formatting | bytes 4194304 | tf_op jit(solution)/shard_map/stack | solution.py:125
  75.0 10.9 %reshape.578 = f32[32,1,16384]{2,1,0:T(1,128)} reshape(f32[4096,1,2,2,32]{4,3,2,1,0:T(2,128)} %bitcast.361) | data formatting | bytes 4194304
  85.8 8.5 %all-to-all-start = ((f32[32,1,16384]{2,1,0:T(1,128)}), f32[32,1,16384]{2,1,0:T(1,128)S(1)}, u32[]{:S(2)}, u32[]{:S(2)}) async-start(f32[32,1,16384]{2,1,0:T(1,128)} %reshape.578), calls=%async_computation | async-start | bytes 4194304 | tf_op jit(solution)/shard_map/all_to_all | solution.py:126
  101.7 2.8 %dynamic-slice_cosine_fusion = (f32[4,1,256,128]{3,2,1,0:T(8,128)S(1)}, f32[4,1,256,128]{3,2,1,0:T(8,128)S(1)}) fusion(f32[8,1,256,128]{3,2,1,0:T(8,128)} %bitcast_dynamic-update-slice_fusion.1, s32[]{:T(128)S(6)} %select_n.195), kind=kLoop, calls=%fused_computation.113 | loop fusion | bytes 1572868 | tf_op jit(solution)/shard_map/cos | solution.py:129
  105.1 19.2 %all-to-all-done = f32[32,1,16384]{2,1,0:T(1,128)S(1)} async-done(((f32[32,1,16384]{2,1,0:T(1,128)}), f32[32,1,16384]{2,1,0:T(1,128)S(1)}, u32[]{:S(2)}, u32[]{:S(2)}) %all-to-all-start) | async-done | bytes 2097184 | tf_op jit(solution)/shard_map/all_to_all | solution.py:126
  126.2 7.4 %reduce.4 = f32[32,16384]{1,0:T(8,128)S(1)} reduce(f32[32,1,16384]{2,1,0:T(1,128)} %copy-done.6, f32[]{:T(128)} %broadcast.762), dimensions={1}, to_apply=%all_to_all.26.reduce_sub_computation | reduce | bytes 4194308 | tf_op jit(solution)/shard_map/all_to_all | solution.py:126
  133.6 8.5 %reshape.579 = f32[4096,1,2,2,32]{4,3,2,1,0:T(2,128)} reshape(f32[32,16384]{1,0:T(8,128)S(1)} %reduce.4) | data formatting | bytes 4194304
  142.1 10.8 %copy.122 = f32[1,2,2,32,4096]{4,0,3,2,1:T(1,128)S(1)} copy(f32[1,2,2,32,4096]{3,1,2,0,4:T(2,128)} %bitcast.362) | data formatting | bytes 4194304 | tf_op jit(solution)/shard_map/all_to_all | solution.py:126
  182.1 3.0 %copy.140 = f32[1,2,2,1024,128]{4,1,2,0,3:T(2,128)} copy(f32[1,2,2,1024,128]{4,3,1,2,0:T(8,128)S(1)} %pad_maximum_fusion.1) | data formatting | bytes 4194304 | tf_op jit(solution)/shard_map/stack | solution.py:144
  185.0 4.0 %all-to-all-start.1 = ((f32[1,2,2,1024,128]{4,1,2,0,3:T(2,128)}), f32[1,2,2,1024,128]{4,1,2,0,3:T(2,128)S(1)}, u32[]{:S(2)}, u32[]{:S(2)}) async-start(f32[1,2,2,1024,128]{4,1,2,0,3:T(2,128)} %copy.140), calls=%async_computation.1 | async-start | bytes 4194304 | tf_op jit(solution)/shard_map/all_to_all | solution.py:145
  189.2 29.8 %all-to-all-done.1 = f32[1,2,2,1024,128]{4,1,2,0,3:T(2,128)S(1)} async-done(((f32[1,2,2,1024,128]{4,1,2,0,3:T(2,128)}), f32[1,2,2,1024,128]{4,1,2,0,3:T(2,128)S(1)}, u32[]{:S(2)}, u32[]{:S(2)}) %all-to-all-start.1) | async-done | bytes 2097184 | tf_op jit(solution)/shard_map/all_to_all | solution.py:145
  220.4 6.4 %slice_reduce_fusion = (f32[2,32,4096]{2,1,0:T(8,128)S(1)}, f32[2,32,4096]{2,1,0:T(8,128)}) fusion(f32[1,2,2,32,4096]{4,0,3,2,1:T(1,128)S(1)} %bitcast.369), kind=kLoop, calls=%fused_computation.59 | loop fusion | bytes 4194304 | tf_op jit(solution)/shard_map/slice | solution.py:99
  226.8 2.4 reshape.556
  229.2 3.3 %fusion.102 = f32[64,2,32,64]{3,0,2,1:T(8,128)} fusion(f32[2,32,64,64]{3,2,1,0:T(8,128)S(1)} %reshape.556), kind=kOutput, calls=%fused_computation.151 | convolution fusion | flops 201383936 | bytes 2097152 | tf_op jit(solution)/shard_map/...nj,nk->...kj/dot_general | solution.py:58
  232.5 3.4 %fusion.86 = f32[64,2,32,64]{3,0,2,1:T(8,128)} fusion(f32[2,32,64,64]{3,2,1,0:T(8,128)S(1)} %reshape.556), kind=kOutput, calls=%fused_computation.135 | convolution fusion | flops 201383936 | bytes 2097152 | tf_op jit(solution)/shard_map/...nj,nk->...kj/dot_general | solution.py:61
  238.1 4.4 %convolution_subtract_fusion = f32[64,2,32,64]{3,0,2,1:T(8,128)S(1)} fusion(f32[64,2,32,64]{3,0,2,1:T(8,128)} %fusion.102, f32[2,32,64,64]{3,2,1,0:T(8,128)} %reshape.557), kind=kOutput, calls=%fused_computation.37 | convolution fusion | flops 201646080 | bytes 3145728 | tf_op jit(solution)/shard_map/...nj,nk->...kj/dot_general | solution.py:60
  246.7 3.5 %fusion = f32[2,32,64,64]{3,2,1,0:T(8,128)} fusion(f32[64,2,32,64]{3,0,2,1:T(8,128)S(1)} %convolution_add_fusion, f32[64,2,32,64]{3,0,2,1:T(8,128)S(1)} %convolution_subtract_fusion, f32[64,64]{1,0:T(8,128)S(1)} %get-tuple-element.31, f32[64,64]{1,0:T(8,128)S(1)} %get-tuple-element.32), kind=kOutput, calls=%fused_computation.4 | convolution fusion | flops 202170368 | bytes 3178496 | tf_op jit(solution)/shard_map/dot_general | solution.py:76
  250.2 3.4 %multiply_bitcast_fusion.1 = f32[1,2,32,64,64]{3,4,2,1,0:T(8,128)} fusion(f32[2,32,64,64]{3,2,1,0:T(8,128)S(1)} %fusion.2, f32[64,2,32,64]{3,0,2,1:T(8,128)S(1)} %convolution_add_fusion, f32[64,2,32,64]{3,0,2,1:T(8,128)S(1)} %convolution_subtract_fusion, f32[64,64]{1,0:T(8,128)S(1)} %get-tuple-element.31, f32[64,64]{1,0:T(8,128)S(1)} %get-tuple-element.32), kind=kOutput, calls=%fused_computation.33 | convolution fusion | flops 202694656 | bytes 4227072 | tf_op jit(solution)/shard_map/dot_general | solution.py:73
  253.6 3.0 %copy.147 = f32[1,2,32,64,64]{4,3,2,1,0:T(8,128)} copy(f32[1,2,32,64,64]{3,4,2,1,0:T(8,128)} %multiply_bitcast_fusion.1) | data formatting | bytes 2097152 | tf_op jit(solution)/shard_map/mul | solution.py:100
  258.7 5.5 %multiply_bitcast_fusion = f32[1,2,32,64,64]{3,4,2,1,0:T(8,128)} fusion(f32[2,32,64,64]{3,2,1,0:T(8,128)} %fusion, f32[64,2,32,64]{3,0,2,1:T(8,128)} %copy-done.1, f32[64,2,32,64]{3,0,2,1:T(8,128)S(1)} %convolution_subtract_fusion, f32[64,64]{1,0:T(8,128)S(1)} %get-tuple-element.31, f32[64,64]{1,0:T(8,128)S(1)} %get-tuple-element.32), kind=kOutput, calls=%fused_computation.32 | convolution fusion | flops 202694656 | bytes 4227072 | tf_op jit(solution)/shard_map/dot_general | solution.py:76
  (87 shorter events, 76.3 us)
Async XLA Ops:
  0.0 21.4 %copy-start.7 = (f32[1,1,2,2,32,3072]{5,4,3,2,1,0:T(8,128)S(1)}, f32[1,1,2,2,32,3072]{5,4,3,2,1,0:T(8,128)}, u32[]{:S(2)}) copy-start(f32[1,1,2,2,32,3072]{5,4,3,2,1,0:T(8,128)} %param.2) | copy-start | bytes 4718596
  0.0 95.2 %collective-permute-start.1 = (f32[1,256,128]{2,1,0:T(8,128)}, f32[1,256,128]{2,1,0:T(8,128)S(1)}, u32[]{:S(2)}, u32[]{:S(2)}) collective-permute-start(f32[1,256,128]{2,1,0:T(8,128)} %param.3), channel_id=1, source_target_pairs={{1,0},{2,1},{3,2},{0,3},{5,4},{6,5},{7,6},{4,7},{9,8},{10,9},{11,1... | collective-permute-start | bytes 393224 | tf_op jit(solution)/shard_map/ppermute | solution.py:19
  0.4 95.5 %collective-permute-start.2 = (f32[1,256,128]{2,1,0:T(8,128)}, f32[1,256,128]{2,1,0:T(8,128)S(1)}, u32[]{:S(2)}, u32[]{:S(2)}) collective-permute-start(f32[1,256,128]{2,1,0:T(8,128)} %param.3), channel_id=1, source_target_pairs={{2,0},{3,1},{0,2},{1,3},{6,4},{7,5},{4,6},{5,7},{10,8},{11,9},{8,1... | collective-permute-start | bytes 393224 | tf_op jit(solution)/shard_map/ppermute | solution.py:19
  3.0 93.5 %collective-permute-start.3 = (f32[1,256,128]{2,1,0:T(8,128)}, f32[1,256,128]{2,1,0:T(8,128)}, u32[]{:S(2)}, u32[]{:S(2)}) collective-permute-start(f32[1,256,128]{2,1,0:T(8,128)} %param.3), channel_id=1, source_target_pairs={{3,0},{0,1},{1,2},{2,3},{7,4},{4,5},{5,6},{6,7},{11,8},{8,9},{9,10... | collective-permute-start | bytes 393224 | tf_op jit(solution)/shard_map/ppermute | solution.py:19
  6.0 15.4 %collective-permute-start = (f32[1,2,2,32,1024]{4,3,2,1,0:T(8,128)S(1)}, f32[1,2,2,32,1024]{4,3,2,1,0:T(8,128)}, u32[]{:S(2)}, u32[]{:S(2)}) collective-permute-start(f32[1,2,2,32,1024]{4,3,2,1,0:T(8,128)S(1)} %slice.32), channel_id=1, source_target_pairs={{0,1},{1,2},{2,3},{4,5},{5,6},{6,7},{8,9},{9,10},{10,11},{12,13},{... | collective-permute-start | bytes 1572872 | tf_op jit(solution)/shard_map/ppermute | solution.py:11
  35.0 4.4 %copy-start.2 = (f32[2,32,64,64]{3,2,1,0:T(8,128)S(1)}, f32[2,32,64,64]{3,2,1,0:T(8,128)}, u32[]{:S(2)}) copy-start(f32[2,32,64,64]{3,2,1,0:T(8,128)} %reshape.540) | copy-start | bytes 3145732
  35.0 4.4 %copy-start.4 = (f32[64,2,32,64]{3,0,2,1:T(8,128)S(1)}, f32[64,2,32,64]{3,0,2,1:T(8,128)}, u32[]{:S(2)}) copy-start(f32[64,2,32,64]{3,0,2,1:T(8,128)} %fusion.96) | copy-start | bytes 3145732
  41.5 5.6 %copy-start = (f32[64,2,32,64]{3,0,2,1:T(8,128)}, f32[64,2,32,64]{3,0,2,1:T(8,128)S(1)}, u32[]{:S(2)}) copy-start(f32[64,2,32,64]{3,0,2,1:T(8,128)S(1)} %convolution_add_fusion.1) | copy-start | bytes 3145732
  85.8 8.5 %copy-start.10 = (f32[1,256,128]{2,1,0:T(8,128)S(1)}, f32[1,256,128]{2,1,0:T(8,128)}, u32[]{:S(2)}) copy-start(f32[1,256,128]{2,1,0:T(8,128)} %param.3) | copy-start | bytes 393220
  85.8 38.5 %all-to-all-start = ((f32[32,1,16384]{2,1,0:T(1,128)}), f32[32,1,16384]{2,1,0:T(1,128)S(1)}, u32[]{:S(2)}, u32[]{:S(2)}) async-start(f32[32,1,16384]{2,1,0:T(1,128)} %reshape.578), calls=%async_computation | async-start | bytes 4194304 | tf_op jit(solution)/shard_map/all_to_all | solution.py:126
  124.3 1.3 copy-start.6
  179.3 2.4 copy-start.8
  179.3 2.4 copy-start.9
  185.0 34.0 %all-to-all-start.1 = ((f32[1,2,2,1024,128]{4,1,2,0,3:T(2,128)}), f32[1,2,2,1024,128]{4,1,2,0,3:T(2,128)S(1)}, u32[]{:S(2)}, u32[]{:S(2)}) async-start(f32[1,2,2,1024,128]{4,1,2,0,3:T(2,128)} %copy.140), calls=%async_computation.1 | async-start | bytes 4194304 | tf_op jit(solution)/shard_map/all_to_all | solution.py:145
  238.1 4.4 %copy-start.3 = (f32[2,32,64,64]{3,2,1,0:T(8,128)S(1)}, f32[2,32,64,64]{3,2,1,0:T(8,128)}, u32[]{:S(2)}) copy-start(f32[2,32,64,64]{3,2,1,0:T(8,128)} %reshape.557) | copy-start | bytes 3145732
  238.1 4.4 %copy-start.5 = (f32[64,2,32,64]{3,0,2,1:T(8,128)S(1)}, f32[64,2,32,64]{3,0,2,1:T(8,128)}, u32[]{:S(2)}) copy-start(f32[64,2,32,64]{3,0,2,1:T(8,128)} %fusion.86) | copy-start | bytes 3145732
  244.6 5.6 %copy-start.1 = (f32[64,2,32,64]{3,0,2,1:T(8,128)}, f32[64,2,32,64]{3,0,2,1:T(8,128)S(1)}, u32[]{:S(2)}) copy-start(f32[64,2,32,64]{3,0,2,1:T(8,128)S(1)} %convolution_add_fusion) | copy-start | bytes 3145732
where the time goes:
time: 275 us; the launch traced here: 270 us
  local copies, waits for them, and re-layouts  93.1 us (34%)
  matrix products  81.4 us (30%)
  waiting for transfers between devices  56.1 us (20%)
  other arithmetic  19.8 us (7%)
  starting transfers between devices  19.4 us (7%)
    all_to_all x1, waiting for transfers between devices, per_device(): lax.all_to_all(columns, 'band', split_axis=3, concat_axis=4, tiled=True)  29.8 us
    unnamed x31, local copies, waits for them, and re-layouts  26.3 us
    all_to_all x1, waiting for transfers between devices, per_device(): lax.all_to_all(stacked, 'band', split_axis=4, concat_axis=3, tiled=True)  19.2 us
    dot_general x4, matrix products, transform_last(): jnp.matmul(first_real, sin_inner, precision=highest)  14.5 us
    all_to_all x3, local copies, waits for them, and re-layouts, per_device(): lax.all_to_all(stacked, 'band', split_axis=4, concat_axis=3, tiled=True)  12.6 us
    dot_general x4, matrix products, transform_last(): jnp.einsum('...nj,nk->...kj', imag_part, sin_outer, precision=highest)  11.3 us
    dot_general x4, matrix products, transform_last(): jnp.matmul(first_imag, cos_inner, precision=highest)  10.5 us
    dot_general x4, matrix products, transform_last(): jnp.einsum('...nj,nk->...kj', real_part, cos_outer, precision=highest)  10.5 us
  transfers between devices with their start and end apart: 6, of which 3 were waited for; matrix products, arithmetic and copies ran while one was open for 31% of the time, Pallas kernels for 0%

commit v1 on v0

--- a/solution.py
+++ b/solution.py
@@ -3,6 +3,7 @@
 import jax.numpy as jnp
 from jax import lax
 from jax.sharding import PartitionSpec as P
+from jax.lax import all_to_all, psum
 
 
 def passed_along(block, axis, distance):
@@ -123,7 +124,16 @@
         -2.0 * math.pi / length,
     )
     stacked = jnp.stack([real_part, imag_part], axis=2)
-    spectra = row_pass(lax.all_to_all(stacked, "band", split_axis=4, concat_axis=3, tiled=True))
+
+    def points_carry(x_local, dim_k, which_dim):
+        return jnp.concatenate(
+            all_to_all(
+                jnp.stack(jnp.split(x_local, psum(1, "band"), axis=dim_k), axis=0), "band", 0, 0
+            ),
+            axis=which_dim,
+        )
+
+    spectra = row_pass(points_carry(stacked, 4, 3))
     real_part, imag_part = (spectra[:, :, 0], spectra[:, :, 1])
     phases = gathered(chirp_phase, "seg", 1)
     cosine = jnp.cos(phases)[:, None]

time: 275 us -> 246 us (0.89)
  local copies, waits for them, and re-layouts: 93.1 us -> 51.8 us
  other arithmetic: 19.8 us -> 32.5 us
    unnamed x31 -> x27, local copies, waits for them, and re-layouts: 26.3 us -> 5.6 us
    unnamed x0 -> x31, other arithmetic: none -> 19.7 us
    all_to_all x3 -> x0, local copies, waits for them, and re-layouts: 12.6 us -> none  [per_device(): lax.all_to_all(stacked, 'band', split_axis=4, concat_axis=3, tiled=True)]
    another operation x4 -> x3, local copies, waits for them, and re-layouts: 15.5 us -> 6.93 us  [the longest x1 8.36 us: per_device(): stacked = jnp.stack([real_part, imag_part], axis=2)]
    all_to_all x1 -> x0, other arithmetic: 7.39 us -> none  [per_device(): lax.all_to_all(stacked, 'band', split_axis=4, concat_axis=3, tiled=True)]
  transfers between devices with their start and end apart: 6 -> 6, of which waited for: 3 -> 3; matrix products, arithmetic and copies ran while one was open for 31% -> 35% of each run, Pallas kernels for 0% -> 0%
where the time goes in v1:
time: 246 us; the launch traced here: 242 us
  matrix products  81.7 us (33%)
  waiting for transfers between devices  55.9 us (23%)
  local copies, waits for them, and re-layouts  51.8 us (21%)
  other arithmetic  32.5 us (13%)
  starting transfers between devices  19.2 us (8%)
    all_to_all x1, waiting for transfers between devices, per_device(): lax.all_to_all(columns, 'band', split_axis=3, concat_axis=4, tiled=True)  29.8 us
    unnamed x31, other arithmetic  19.7 us
    all_to_all x1, waiting for transfers between devices, points_carry(): all_to_all(jnp.stack(jnp.split(x_local, psum(1, 'band'), axis=dim_k), axi...  19 us
    dot_general x4, matrix products, transform_last(): jnp.matmul(first_real, sin_inner, precision=highest)  14.4 us
    dot_general x4, matrix products, transform_last(): jnp.einsum('...nj,nk->...kj', imag_part, sin_outer, precision=highest)  11.3 us
    dot_general x4, matrix products, transform_last(): jnp.matmul(first_imag, cos_inner, precision=highest)  10.6 us
    dot_general x4, matrix products, transform_last(): jnp.einsum('...nj,nk->...kj', real_part, cos_outer, precision=highest)  10.4 us
    dot_general x4, matrix products, transform_last(): jnp.matmul(first_real, cos_inner, precision=highest)  10.2 us
  transfers between devices with their start and end apart: 6, of which 3 were waited for; matrix products, arithmetic and copies ran while one was open for 35% of the time, Pallas kernels for 0%

profile of v1, /device:TPU:8, one launch (start us, length us, event | category | flops | bytes accessed | tf_op | source)
XLA Modules:
  0.0 241.9 jit_solution(8297500860540753426)
XLA Ops:
  0.4 2.7 %collective-permute-start.2 = (f32[1,256,128]{2,1,0:T(8,128)}, f32[1,256,128]{2,1,0:T(8,128)S(1)}, u32[]{:S(2)}, u32[]{:S(2)}) collective-permute-start(f32[1,256,128]{2,1,0:T(8,128)} %param.3), channel_id=1, source_target_pairs={{2,0},{3,1},{0,2},{1,3},{6,4},{7,5},{4,6},{5,7},{10,8},{11,9},{8,1... | collective-permute-start | bytes 393224 | tf_op jit(solution)/shard_map/ppermute | solution.py:20
  8.0 3.3 %fusion.81 = (f32[32,4096]{1,0:T(8,128)}, f32[32,4096]{1,0:T(8,128)}) fusion(s32[32]{0:T(128)S(1)} %iota_add_fusion.1), kind=kLoop, calls=%fused_computation.178 | loop fusion | flops 1835008 | bytes 1048704 | tf_op jit(solution)/shard_map/cos | solution.py:45
  11.4 2.9 %fusion.79 = (f32[1024,128]{1,0:T(8,128)}, f32[1024,128]{1,0:T(8,128)}) fusion(s32[128]{0:T(128)S(1)} %iota_add_fusion), kind=kLoop, calls=%fused_computation.176 | loop fusion | flops 1835008 | bytes 1049088 | tf_op jit(solution)/shard_map/cos | solution.py:45
  14.3 7.1 %collective-permute-done = f32[1,2,2,32,1024]{4,3,2,1,0:T(8,128)} collective-permute-done((f32[1,2,2,32,1024]{4,3,2,1,0:T(8,128)S(1)}, f32[1,2,2,32,1024]{4,3,2,1,0:T(8,128)}, u32[]{:S(2)}, u32[]{:S(2)}) %collective-permute-start) | collective-permute-done | bytes 524320 | tf_op jit(solution)/shard_map/ppermute | solution.py:12
  21.4 2.2 fusion.37
  23.6 2.5 %reshape.547 = f32[2,32,64,64]{3,2,1,0:T(8,128)S(1)} reshape(f32[1,2,1,32,4096]{4,3,2,1,0:T(8,128)} %get-tuple-element.18) | data formatting | bytes 2097152 | tf_op jit(solution)/shard_map/reshape.2
  26.1 3.3 %fusion.124 = f32[64,2,32,64]{3,0,2,1:T(8,128)} fusion(f32[2,32,64,64]{3,2,1,0:T(8,128)S(1)} %reshape.547), kind=kOutput, calls=%fused_computation.267 | convolution fusion | flops 201383936 | bytes 2097152 | tf_op jit(solution)/shard_map/...nj,nk->...kj/dot_general | solution.py:61
  29.4 3.4 %fusion.128 = f32[64,2,32,64]{3,0,2,1:T(8,128)} fusion(f32[2,32,64,64]{3,2,1,0:T(8,128)S(1)} %reshape.547), kind=kOutput, calls=%fused_computation.271 | convolution fusion | flops 201383936 | bytes 2097152 | tf_op jit(solution)/shard_map/...nj,nk->...kj/dot_general | solution.py:64
  32.8 2.2 reshape.546
  35.0 4.4 %convolution_subtract_fusion.1 = f32[64,2,32,64]{3,0,2,1:T(8,128)S(1)} fusion(f32[64,2,32,64]{3,0,2,1:T(8,128)} %fusion.124, f32[2,32,64,64]{3,2,1,0:T(8,128)} %reshape.546), kind=kOutput, calls=%fused_computation.100 | convolution fusion | flops 201646080 | bytes 3145728 | tf_op jit(solution)/shard_map/...nj,nk->...kj/dot_general | solution.py:59
  43.6 3.5 %fusion.10 = f32[2,32,64,64]{3,2,1,0:T(8,128)} fusion(f32[64,2,32,64]{3,0,2,1:T(8,128)S(1)} %convolution_add_fusion.1, f32[64,2,32,64]{3,0,2,1:T(8,128)S(1)} %convolution_subtract_fusion.1, f32[64,64]{1,0:T(8,128)S(1)} %get-tuple-element.25, f32[64,64]{1,0:T(8,128)S(1)} %get-tuple-element.26), kind=kOutput, calls=%fused_computation.79 | convolution fusion | flops 202170368 | bytes 3178496 | tf_op jit(solution)/shard_map/dot_general | solution.py:77
  47.1 3.4 %subtract_bitcast_fusion = f32[1,2,32,64,64]{3,4,2,1,0:T(8,128)} fusion(f32[2,32,64,64]{3,2,1,0:T(8,128)S(1)} %fusion.12, f32[64,2,32,64]{3,0,2,1:T(8,128)S(1)} %convolution_add_fusion.1, f32[64,2,32,64]{3,0,2,1:T(8,128)S(1)} %convolution_subtract_fusion.1, f32[64,64]{1,0:T(8,128)S(1)} %get-tuple-element.25, f32[64,64]{1,0:T(8,128)S(1)} %get-tuple-element.26), kind=kOutput, calls=%fused_computation.96 | convolution fusion | flops 202432512 | bytes 4227072 | tf_op jit(solution)/shard_map/dot_general | solution.py:74
  50.5 3.0 %copy.86 = f32[1,2,32,64,64]{4,3,2,1,0:T(8,128)} copy(f32[1,2,32,64,64]{3,4,2,1,0:T(8,128)} %subtract_bitcast_fusion) | data formatting | bytes 2097152 | tf_op jit(solution)/shard_map/transpose | solution.py:80
  53.5 2.1 reshape.550
  55.6 5.5 %add_bitcast_fusion = f32[1,2,32,64,64]{3,4,2,1,0:T(8,128)} fusion(f32[2,32,64,64]{3,2,1,0:T(8,128)} %fusion.10, f32[64,2,32,64]{3,0,2,1:T(8,128)} %copy-done, f32[64,2,32,64]{3,0,2,1:T(8,128)S(1)} %convolution_subtract_fusion.1, f32[64,64]{1,0:T(8,128)S(1)} %get-tuple-element.25, f32[64,64]{1,0:T(8,128)S(1)} %get-tuple-element.26), kind=kOutput, calls=%fused_computation.95 | convolution fusion | flops 202432512 | bytes 4227072 | tf_op jit(solution)/shard_map/dot_general | solution.py:77
  86.8 8.3 %all-to-all-start = ((f32[32,1,2,2,32,128]{5,4,2,3,1,0:T(8,128)}), f32[32,1,2,2,32,128]{5,4,2,3,1,0:T(8,128)S(1)}, u32[]{:S(2)}, u32[]{:S(2)}) async-start(f32[32,1,2,2,32,128]{5,4,2,3,1,0:T(8,128)} %constant_dynamic-update-slice_fusion), calls=%async_computation | async-start | bytes 4194304 | tf_op jit(solution)/shard_map/all_to_all | solution.py:130
  102.5 3.0 %dynamic-slice_cosine_fusion = (f32[4,1,256,128]{3,2,1,0:T(8,128)S(1)}, f32[4,1,256,128]{3,2,1,0:T(8,128)S(1)}) fusion(f32[8,1,256,128]{3,2,1,0:T(8,128)} %bitcast_dynamic-update-slice_fusion.1, s32[]{:T(128)S(6)} %select_n.195), kind=kLoop, calls=%fused_computation.174 | loop fusion | bytes 1572868 | tf_op jit(solution)/shard_map/cos | solution.py:139
  106.1 19.0 %all-to-all-done = f32[32,1,2,2,32,128]{5,4,2,3,1,0:T(8,128)S(1)} async-done(((f32[32,1,2,2,32,128]{5,4,2,3,1,0:T(8,128)}), f32[32,1,2,2,32,128]{5,4,2,3,1,0:T(8,128)S(1)}, u32[]{:S(2)}, u32[]{:S(2)}) %all-to-all-start) | async-done | bytes 2097184 | tf_op jit(solution)/shard_map/all_to_all | solution.py:130
  135.8 2.2 fusion.34
  153.5 2.9 %copy.105 = f32[1,2,2,1024,128]{4,1,2,0,3:T(2,128)} copy(f32[1,2,2,1024,128]{4,3,1,2,0:T(8,128)S(1)} %pad_maximum_fusion) | data formatting | bytes 4194304 | tf_op jit(solution)/shard_map/stack | solution.py:154
  156.4 4.0 %all-to-all-start.1 = ((f32[1,2,2,1024,128]{4,1,2,0,3:T(2,128)}), f32[1,2,2,1024,128]{4,1,2,0,3:T(2,128)S(1)}, u32[]{:S(2)}, u32[]{:S(2)}) async-start(f32[1,2,2,1024,128]{4,1,2,0,3:T(2,128)} %copy.105), calls=%async_computation.1 | async-start | bytes 4194304 | tf_op jit(solution)/shard_map/all_to_all | solution.py:155
  160.6 29.8 %all-to-all-done.1 = f32[1,2,2,1024,128]{4,1,2,0,3:T(2,128)S(1)} async-done(((f32[1,2,2,1024,128]{4,1,2,0,3:T(2,128)}), f32[1,2,2,1024,128]{4,1,2,0,3:T(2,128)S(1)}, u32[]{:S(2)}, u32[]{:S(2)}) %all-to-all-start.1) | async-done | bytes 2097184 | tf_op jit(solution)/shard_map/all_to_all | solution.py:155
  191.8 6.4 %slice_reduce_fusion = (f32[2,32,4096]{2,1,0:T(8,128)S(1)}, f32[2,32,4096]{2,1,0:T(8,128)}) fusion(f32[1,2,2,32,4096]{4,0,3,2,1:T(1,128)S(1)} %bitcast.429), kind=kLoop, calls=%fused_computation.120 | loop fusion | bytes 4194304 | tf_op jit(solution)/shard_map/slice | solution.py:100
  198.2 2.2 reshape.564
  200.4 3.3 %fusion.134 = f32[64,2,32,64]{3,0,2,1:T(8,128)} fusion(f32[2,32,64,64]{3,2,1,0:T(8,128)S(1)} %reshape.564), kind=kOutput, calls=%fused_computation.277 | convolution fusion | flops 201383936 | bytes 2097152 | tf_op jit(solution)/shard_map/...nj,nk->...kj/dot_general | solution.py:59
  203.8 3.4 %fusion.118 = f32[64,2,32,64]{3,0,2,1:T(8,128)} fusion(f32[2,32,64,64]{3,2,1,0:T(8,128)S(1)} %reshape.564), kind=kOutput, calls=%fused_computation.261 | convolution fusion | flops 201383936 | bytes 2097152 | tf_op jit(solution)/shard_map/...nj,nk->...kj/dot_general | solution.py:62
  207.1 2.2 reshape.565
  209.3 4.4 %convolution_subtract_fusion = f32[64,2,32,64]{3,0,2,1:T(8,128)S(1)} fusion(f32[64,2,32,64]{3,0,2,1:T(8,128)} %fusion.134, f32[2,32,64,64]{3,2,1,0:T(8,128)} %reshape.565), kind=kOutput, calls=%fused_computation.98 | convolution fusion | flops 201646080 | bytes 3145728 | tf_op jit(solution)/shard_map/...nj,nk->...kj/dot_general | solution.py:61
  218.0 3.6 %fusion = f32[2,32,64,64]{3,2,1,0:T(8,128)} fusion(f32[64,2,32,64]{3,0,2,1:T(8,128)S(1)} %convolution_add_fusion, f32[64,2,32,64]{3,0,2,1:T(8,128)S(1)} %convolution_subtract_fusion, f32[64,64]{1,0:T(8,128)S(1)} %get-tuple-element.31, f32[64,64]{1,0:T(8,128)S(1)} %get-tuple-element.32), kind=kOutput, calls=%fused_computation.65 | convolution fusion | flops 202170368 | bytes 3178496 | tf_op jit(solution)/shard_map/dot_general | solution.py:77
  221.5 3.4 %multiply_bitcast_fusion.1 = f32[1,2,32,64,64]{3,4,2,1,0:T(8,128)} fusion(f32[2,32,64,64]{3,2,1,0:T(8,128)S(1)} %fusion.2, f32[64,2,32,64]{3,0,2,1:T(8,128)S(1)} %convolution_add_fusion, f32[64,2,32,64]{3,0,2,1:T(8,128)S(1)} %convolution_subtract_fusion, f32[64,64]{1,0:T(8,128)S(1)} %get-tuple-element.31, f32[64,64]{1,0:T(8,128)S(1)} %get-tuple-element.32), kind=kOutput, calls=%fused_computation.94 | convolution fusion | flops 202694656 | bytes 4227072 | tf_op jit(solution)/shard_map/dot_general | solution.py:74
  224.9 3.0 %copy.112 = f32[1,2,32,64,64]{4,3,2,1,0:T(8,128)} copy(f32[1,2,32,64,64]{3,4,2,1,0:T(8,128)} %multiply_bitcast_fusion.1) | data formatting | bytes 2097152 | tf_op jit(solution)/shard_map/mul | solution.py:101
  230.1 5.5 %multiply_bitcast_fusion = f32[1,2,32,64,64]{3,4,2,1,0:T(8,128)} fusion(f32[2,32,64,64]{3,2,1,0:T(8,128)} %fusion, f32[64,2,32,64]{3,0,2,1:T(8,128)} %copy-done.1, f32[64,2,32,64]{3,0,2,1:T(8,128)S(1)} %convolution_subtract_fusion, f32[64,64]{1,0:T(8,128)S(1)} %get-tuple-element.31, f32[64,64]{1,0:T(8,128)S(1)} %get-tuple-element.32), kind=kOutput, calls=%fused_computation.93 | convolution fusion | flops 202694656 | bytes 4227072 | tf_op jit(solution)/shard_map/dot_general | solution.py:77
  (110 shorter events, 83.0 us)
Async XLA Ops:
  0.0 21.4 %copy-start.6 = (f32[1,1,2,2,32,3072]{5,4,3,2,1,0:T(8,128)S(1)}, f32[1,1,2,2,32,3072]{5,4,3,2,1,0:T(8,128)}, u32[]{:S(2)}) copy-start(f32[1,1,2,2,32,3072]{5,4,3,2,1,0:T(8,128)} %param.2) | copy-start | bytes 4718596
  0.0 96.0 %collective-permute-start.1 = (f32[1,256,128]{2,1,0:T(8,128)}, f32[1,256,128]{2,1,0:T(8,128)S(1)}, u32[]{:S(2)}, u32[]{:S(2)}) collective-permute-start(f32[1,256,128]{2,1,0:T(8,128)} %param.3), channel_id=1, source_target_pairs={{1,0},{2,1},{3,2},{0,3},{5,4},{6,5},{7,6},{4,7},{9,8},{10,9},{11,1... | collective-permute-start | bytes 393224 | tf_op jit(solution)/shard_map/ppermute | solution.py:20
  0.4 96.3 %collective-permute-start.2 = (f32[1,256,128]{2,1,0:T(8,128)}, f32[1,256,128]{2,1,0:T(8,128)S(1)}, u32[]{:S(2)}, u32[]{:S(2)}) collective-permute-start(f32[1,256,128]{2,1,0:T(8,128)} %param.3), channel_id=1, source_target_pairs={{2,0},{3,1},{0,2},{1,3},{6,4},{7,5},{4,6},{5,7},{10,8},{11,9},{8,1... | collective-permute-start | bytes 393224 | tf_op jit(solution)/shard_map/ppermute | solution.py:20
  3.0 94.3 %collective-permute-start.3 = (f32[1,256,128]{2,1,0:T(8,128)}, f32[1,256,128]{2,1,0:T(8,128)}, u32[]{:S(2)}, u32[]{:S(2)}) collective-permute-start(f32[1,256,128]{2,1,0:T(8,128)} %param.3), channel_id=1, source_target_pairs={{3,0},{0,1},{1,2},{2,3},{7,4},{4,5},{5,6},{6,7},{11,8},{8,9},{9,10... | collective-permute-start | bytes 393224 | tf_op jit(solution)/shard_map/ppermute | solution.py:20
  6.0 15.4 %collective-permute-start = (f32[1,2,2,32,1024]{4,3,2,1,0:T(8,128)S(1)}, f32[1,2,2,32,1024]{4,3,2,1,0:T(8,128)}, u32[]{:S(2)}, u32[]{:S(2)}) collective-permute-start(f32[1,2,2,32,1024]{4,3,2,1,0:T(8,128)S(1)} %slice.32), channel_id=1, source_target_pairs={{0,1},{1,2},{2,3},{4,5},{5,6},{6,7},{8,9},{9,10},{10,11},{12,13},{... | collective-permute-start | bytes 1572872 | tf_op jit(solution)/shard_map/ppermute | solution.py:12
  35.0 4.4 %copy-start.2 = (f32[2,32,64,64]{3,2,1,0:T(8,128)S(1)}, f32[2,32,64,64]{3,2,1,0:T(8,128)}, u32[]{:S(2)}) copy-start(f32[2,32,64,64]{3,2,1,0:T(8,128)} %reshape.546) | copy-start | bytes 3145732
  35.0 4.4 %copy-start.4 = (f32[64,2,32,64]{3,0,2,1:T(8,128)S(1)}, f32[64,2,32,64]{3,0,2,1:T(8,128)}, u32[]{:S(2)}) copy-start(f32[64,2,32,64]{3,0,2,1:T(8,128)} %fusion.128) | copy-start | bytes 3145732
  41.5 5.6 %copy-start = (f32[64,2,32,64]{3,0,2,1:T(8,128)}, f32[64,2,32,64]{3,0,2,1:T(8,128)S(1)}, u32[]{:S(2)}) copy-start(f32[64,2,32,64]{3,0,2,1:T(8,128)S(1)} %convolution_add_fusion.1) | copy-start | bytes 3145732
  86.8 8.3 %copy-start.9 = (f32[1,256,128]{2,1,0:T(8,128)S(1)}, f32[1,256,128]{2,1,0:T(8,128)}, u32[]{:S(2)}) copy-start(f32[1,256,128]{2,1,0:T(8,128)} %param.3) | copy-start | bytes 393220
  86.8 38.3 %all-to-all-start = ((f32[32,1,2,2,32,128]{5,4,2,3,1,0:T(8,128)}), f32[32,1,2,2,32,128]{5,4,2,3,1,0:T(8,128)S(1)}, u32[]{:S(2)}, u32[]{:S(2)}) async-start(f32[32,1,2,2,32,128]{5,4,2,3,1,0:T(8,128)} %constant_dynamic-update-slice_fusion), calls=%async_computation | async-start | bytes 4194304 | tf_op jit(solution)/shard_map/all_to_all | solution.py:130
  150.7 2.4 copy-start.7
  150.8 2.4 copy-start.8
  156.4 34.0 %all-to-all-start.1 = ((f32[1,2,2,1024,128]{4,1,2,0,3:T(2,128)}), f32[1,2,2,1024,128]{4,1,2,0,3:T(2,128)S(1)}, u32[]{:S(2)}, u32[]{:S(2)}) async-start(f32[1,2,2,1024,128]{4,1,2,0,3:T(2,128)} %copy.105), calls=%async_computation.1 | async-start | bytes 4194304 | tf_op jit(solution)/shard_map/all_to_all | solution.py:155
  209.3 4.4 %copy-start.3 = (f32[2,32,64,64]{3,2,1,0:T(8,128)S(1)}, f32[2,32,64,64]{3,2,1,0:T(8,128)}, u32[]{:S(2)}) copy-start(f32[2,32,64,64]{3,2,1,0:T(8,128)} %reshape.565) | copy-start | bytes 3145732
  209.3 4.4 %copy-start.5 = (f32[64,2,32,64]{3,0,2,1:T(8,128)S(1)}, f32[64,2,32,64]{3,0,2,1:T(8,128)}, u32[]{:S(2)}) copy-start(f32[64,2,32,64]{3,0,2,1:T(8,128)} %fusion.118) | copy-start | bytes 3145732
  215.8 5.7 %copy-start.1 = (f32[64,2,32,64]{3,0,2,1:T(8,128)}, f32[64,2,32,64]{3,0,2,1:T(8,128)S(1)}, u32[]{:S(2)}) copy-start(f32[64,2,32,64]{3,0,2,1:T(8,128)S(1)} %convolution_add_fusion) | copy-start | bytes 3145732
